TPU v7x, 32 devices: a whole 2x2x4 slice. The times are simulated.
32 devices in a mesh: row: 4 (over y, x), col: 8 (over z, core).
Axes of the slice: x: 2, y: 2, z: 4, core: 2. Of those that a mesh axis runs over, the one named last changes fastest.
Arguments:
- density: float32 [2048, 2048], P('row', 'col'), as said below
- pattern: int32 [16, 16], replicated, may hold values from 0 to 1, as said below
Outputs:
- purified: float32 [2048, 2048], P('row', 'col')
Inputs may be any that keep to these rules, and one draw needn't show every extreme that they name: density is symmetric and zero outside the blocks that pattern allows. pattern is symmetric with ones on its diagonal, and every block row holds exactly 7 ones.
All inputs are finite; a program needn't handle non-finite values.
Results may differ from a plain program's by a relative error of at most 0.0061.
Values may be sent and summed in bfloat16 or wider, within the bound.
No kernel may reach another device: no remote copies, remote signals or barrier semaphores. Data moves between devices by JAX's collectives and lax.ppermute only.
A program may use at most 64 MiB of HBM per device.

v0:
```python
import jax
import jax.numpy as jnp
from jax import lax
from jax.sharding import PartitionSpec as P

BS = 128
STEPS = 2


def allowed_blocks(pattern):
    count = pattern.shape[0]
    index = lax.iota(jnp.int32, count)
    eye = (index[:, None] == index[None, :]).astype(jnp.int32)
    return jnp.maximum(jnp.maximum(pattern, pattern.T), eye)


def apply_mask(values, blocks):
    row_blocks, col_blocks = blocks.shape
    shaped = values.reshape(row_blocks, BS, col_blocks, BS) * blocks[:, None, :, None]
    return shaped.reshape(row_blocks * BS, col_blocks * BS)


def on_device(density, pattern):
    rows, cols = density.shape
    row_blocks = rows // BS
    col_blocks = cols // BS
    allowed = allowed_blocks(pattern)
    first_row = lax.axis_index("row") * row_blocks
    first_col = lax.axis_index("col") * col_blocks
    blocks = lax.dynamic_slice(allowed, (first_row, first_col), (row_blocks, col_blocks)).astype(
        jnp.float32
    )
    current = apply_mask(density, blocks)
    for step in range(STEPS):
        xb = current.astype(jnp.bfloat16)
        x_panel = lax.all_gather(xb, "row", axis=0, tiled=True)
        square = jnp.dot(
            lax.all_gather(xb, "col", axis=1, tiled=True),
            x_panel,
            preferred_element_type=jnp.float32,
        )
        square = apply_mask(square, blocks)
        qb = square.astype(jnp.bfloat16)
        q_panel = lax.all_gather(qb, "row", axis=0, tiled=True)
        total = jnp.dot(
            lax.all_gather(qb, "col", axis=1, tiled=True),
            x_panel,
            preferred_element_type=jnp.float32,
        )
        jordan = total + jnp.dot(
            lax.all_gather(xb, "col", axis=1, tiled=True),
            q_panel,
            preferred_element_type=jnp.float32,
        )
        current = apply_mask(3.0 * square - jordan, blocks)
    return current


def solution(mesh):
    placed = (P("row", "col"), P())
    return jax.shard_map(
        on_device, mesh=mesh, in_specs=placed, out_specs=P("row", "col"), check_vma=False
    )
```

profile of v0, /device:TPU:0, one launch (start us, length us, event | category | flops | bytes accessed | tf_op | source)
XLA Modules:
  0.0 265.3 jit_solution(4661226299853887989)
XLA Ops:
  6.5 0.8 copy.3
  7.3 0.8 fusion.7
  8.1 0.2 mul.53
  8.3 1.8 fusion.5
  10.1 0.0 all-gather.9.cloned.1.call-start
  10.2 0.7 all-gather.9.cloned.1.call-update
  10.9 28.7 %all-gather.11.cloned.1.call-done = bf16[2048,256]{1,0:T(8,128)(2,1)} async-done(((bf16[512,256]{1,0:T(8,128)(2,1)}), bf16[2048,256]{1,0:T(8,128)(2,1)}) %all-gather.11.cloned.1.call-update) | async-done | bytes 1048592 | tf_op jit(solution)/shard_map/all_gather | solution.py:36
  39.6 32.5 %all-gather.9.cloned.1.call-done = bf16[512,2048]{1,0:T(8,128)(2,1)} async-done(((bf16[512,256]{1,0:T(8,128)(2,1)}), bf16[512,2048]{1,0:T(8,128)(2,1)}) %all-gather.9.cloned.1.call-update) | async-done | bytes 2097168 | tf_op jit(solution)/shard_map/all_gather | solution.py:38
  72.0 3.3 %fusion.8 = (bf16[512,256]{1,0:T(8,128)(2,1)}, f32[512,256]{1,0:T(8,128)S(1)}) fusion(f32[64,8,2,128]{3,2,1,0:T(2,128)S(1)} %bitcast.24, bf16[512,2048]{1,0:T(8,128)(2,1)} %all-gather.9.cloned.1.call-done, bf16[2048,256]{1,0:T(8,128)(2,1)} %all-gather.11.cloned.1.call-done), kind=kOutput, calls=%fused_computation.15 | convolution fusion | flops 537133056 | bytes 4456448 | tf_op jit(solution)/shard_map/dot_general | solution.py:37
  75.4 0.5 all-gather.15.cloned.1.call-update
  76.0 29.4 %all-gather.13.cloned.1.call-done = bf16[512,2048]{1,0:T(8,128)(2,1)} async-done(((bf16[512,256]{1,0:T(8,128)(2,1)}), bf16[512,2048]{1,0:T(8,128)(2,1)}) %all-gather.13.cloned.1.call-update) | async-done | bytes 2097168 | tf_op jit(solution)/shard_map/all_gather | solution.py:46
  105.4 3.4 %fusion.10 = f32[512,256]{1,0:T(8,128)} fusion(bf16[512,2048]{1,0:T(8,128)(2,1)} %all-gather.13.cloned.1.call-done, bf16[2048,256]{1,0:T(8,128)(2,1)} %all-gather.11.cloned.1.call-done), kind=kOutput, calls=%fused_computation.17 | convolution fusion | flops 536870912 | bytes 3670016 | tf_op jit(solution)/shard_map/dot_general | solution.py:45
  108.8 24.1 %all-gather.15.cloned.1.call-done = bf16[2048,256]{1,0:T(8,128)(2,1)} async-done(((bf16[512,256]{1,0:T(8,128)(2,1)}), bf16[2048,256]{1,0:T(8,128)(2,1)}) %all-gather.15.cloned.1.call-update) | async-done | bytes 1048592 | tf_op jit(solution)/shard_map/all_gather | solution.py:44
  132.8 2.8 %fusion.4 = bf16[512,256]{1,0:T(8,128)(2,1)} fusion(f32[512,256]{1,0:T(8,128)} %fusion.10, bf16[512,2048]{1,0:T(8,128)(2,1)S(1)} %copy-done.1, bf16[2048,256]{1,0:T(8,128)(2,1)} %all-gather.15.cloned.1.call-done, f32[512,256]{1,0:T(8,128)S(1)} %get-tuple-element.6, f32[64,8,2,128]{3,2,1,0:T(2,128)S(1)} %bitcast.25), kind=kOutput, calls=%fused_computation.8 | convolution fusion | flops 537526272 | bytes 4980736 | tf_op jit(solution)/shard_map/dot_general | solution.py:50
  135.7 0.5 all-gather.17.cloned.1.call-update
  136.2 26.1 %all-gather.19.cloned.1.call-done = bf16[2048,256]{1,0:T(8,128)(2,1)} async-done(((bf16[512,256]{1,0:T(8,128)(2,1)}), bf16[2048,256]{1,0:T(8,128)(2,1)}) %all-gather.19.cloned.1.call-update) | async-done | bytes 1048592 | tf_op jit(solution)/shard_map/all_gather | solution.py:36
  162.4 32.3 %all-gather.17.cloned.1.call-done = bf16[512,2048]{1,0:T(8,128)(2,1)} async-done(((bf16[512,256]{1,0:T(8,128)(2,1)}), bf16[512,2048]{1,0:T(8,128)(2,1)}) %all-gather.17.cloned.1.call-update) | async-done | bytes 2097168 | tf_op jit(solution)/shard_map/all_gather | solution.py:38
  194.7 3.3 %fusion.9 = (bf16[512,256]{1,0:T(8,128)(2,1)}, f32[512,256]{1,0:T(8,128)S(1)}) fusion(f32[64,8,2,128]{3,2,1,0:T(2,128)S(1)} %bitcast.26, bf16[512,2048]{1,0:T(8,128)(2,1)} %all-gather.17.cloned.1.call-done, bf16[2048,256]{1,0:T(8,128)(2,1)} %all-gather.19.cloned.1.call-done), kind=kOutput, calls=%fused_computation.16 | convolution fusion | flops 537133056 | bytes 4456448 | tf_op jit(solution)/shard_map/dot_general | solution.py:37
  198.0 0.0 all-gather.23.cloned.1.call-start
  198.1 0.7 all-gather.23.cloned.1.call-update
  198.8 29.3 %all-gather.21.cloned.1.call-done = bf16[512,2048]{1,0:T(8,128)(2,1)} async-done(((bf16[512,256]{1,0:T(8,128)(2,1)}), bf16[512,2048]{1,0:T(8,128)(2,1)}) %all-gather.21.cloned.1.call-update) | async-done | bytes 2097168 | tf_op jit(solution)/shard_map/all_gather | solution.py:46
  228.1 3.4 %fusion.11 = f32[512,256]{1,0:T(8,128)} fusion(bf16[512,2048]{1,0:T(8,128)(2,1)} %all-gather.21.cloned.1.call-done, bf16[2048,256]{1,0:T(8,128)(2,1)} %all-gather.19.cloned.1.call-done), kind=kOutput, calls=%fused_computation.18 | convolution fusion | flops 536870912 | bytes 3670016 | tf_op jit(solution)/shard_map/dot_general | solution.py:45
  231.4 24.2 %all-gather.23.cloned.1.call-done = bf16[2048,256]{1,0:T(8,128)(2,1)} async-done(((bf16[512,256]{1,0:T(8,128)(2,1)}), bf16[2048,256]{1,0:T(8,128)(2,1)}) %all-gather.23.cloned.1.call-update) | async-done | bytes 1048592 | tf_op jit(solution)/shard_map/all_gather | solution.py:44
  255.6 2.9 %fusion.3 = f32[512,256]{1,0:T(8,128)} fusion(f32[512,256]{1,0:T(8,128)} %fusion.11, bf16[512,2048]{1,0:T(8,128)(2,1)S(1)} %copy-done, bf16[2048,256]{1,0:T(8,128)(2,1)} %all-gather.23.cloned.1.call-done, f32[512,256]{1,0:T(8,128)S(1)} %get-tuple-element.8, f32[64,8,2,128]{3,2,1,0:T(2,128)S(1)} %bitcast.27), kind=kOutput, calls=%fused_computation.7 | convolution fusion | flops 537395200 | bytes 5242880 | tf_op jit(solution)/shard_map/dot_general | solution.py:50
  (14 shorter events, 0.3 us)
Async XLA Ops:
  6.5 33.0 %all-gather.11.cloned.1.call-start = ((), (), s32[]{:S(2)}) async-start(), calls=%async_computation.1 | async-start | bytes 1310720 | tf_op jit(solution)/shard_map/all_gather | solution.py:36
  10.1 61.9 %all-gather.9.cloned.1.call-start = ((), (), s32[]{:S(2)}) async-start(), calls=%async_computation | async-start | bytes 2359296 | tf_op jit(solution)/shard_map/all_gather | solution.py:38
  10.9 94.5 %all-gather.13.cloned.1.call-start = ((), (), s32[]{:S(2)}) async-start(), calls=%async_computation.2 | async-start | bytes 2359296 | tf_op jit(solution)/shard_map/all_gather | solution.py:46
  75.3 57.5 %copy-start.1 = (bf16[512,2048]{1,0:T(8,128)(2,1)S(1)}, bf16[512,2048]{1,0:T(8,128)(2,1)}, u32[]{:S(2)}) copy-start(bf16[512,2048]{1,0:T(8,128)(2,1)} %all-gather.9.cloned.1.call-done) | copy-start | bytes 6291460
  75.3 57.5 %all-gather.15.cloned.1.call-start = ((), (), s32[]{:S(2)}) async-start(), calls=%async_computation.3 | async-start | bytes 1310720 | tf_op jit(solution)/shard_map/all_gather | solution.py:44
  75.9 86.5 %all-gather.19.cloned.1.call-start = ((), (), s32[]{:S(2)}) async-start(), calls=%async_computation.5 | async-start | bytes 1310720 | tf_op jit(solution)/shard_map/all_gather | solution.py:36
  135.6 59.1 %all-gather.17.cloned.1.call-start = ((), (), s32[]{:S(2)}) async-start(), calls=%async_computation.4 | async-start | bytes 2359296 | tf_op jit(solution)/shard_map/all_gather | solution.py:38
  136.2 91.9 %all-gather.21.cloned.1.call-start = ((), (), s32[]{:S(2)}) async-start(), calls=%async_computation.6 | async-start | bytes 2359296 | tf_op jit(solution)/shard_map/all_gather | solution.py:46
  198.0 57.6 %copy-start = (bf16[512,2048]{1,0:T(8,128)(2,1)S(1)}, bf16[512,2048]{1,0:T(8,128)(2,1)}, u32[]{:S(2)}) copy-start(bf16[512,2048]{1,0:T(8,128)(2,1)} %all-gather.17.cloned.1.call-done) | copy-start | bytes 6291460
  198.0 57.6 %all-gather.23.cloned.1.call-start = ((), (), s32[]{:S(2)}) async-start(), calls=%async_computation.7 | async-start | bytes 1310720 | tf_op jit(solution)/shard_map/all_gather | solution.py:44
Sparse Core Ops, SparseCore 0:
  10.2 29.3 all-gather.10
  41.2 30.8 all-gather.8
  75.5 29.8 all-gather.12
  107.1 25.6 all-gather.14
  135.7 26.6 all-gather.18
  163.8 30.8 all-gather.16
  198.1 29.8 all-gather.20
  229.9 25.6 all-gather.22
where the time goes:
time: 266 us; the launch traced here: 265 us
  waiting for transfers between devices  229 us (86%)
  matrix products  18.9 us (7%)
  between operations  13.5 us (5%)
    all_gather x2, waiting for transfers between devices, on_device(): lax.all_gather(xb, 'col', axis=1, tiled=True)  64.8 us
    all_gather x2, waiting for transfers between devices, on_device(): lax.all_gather(qb, 'col', axis=1, tiled=True)  58.7 us
    all_gather x2, waiting for transfers between devices, on_device(): x_panel = lax.all_gather(xb, 'row', axis=0, tiled=True)  54.8 us
    all_gather x2, waiting for transfers between devices, on_device(): q_panel = lax.all_gather(qb, 'row', axis=0, tiled=True)  48.3 us
    dot_general x2, matrix products, on_device(): jnp.dot(lax.all_gather(qb, 'col', axis=1, tiled=True), x_panel, preferred...  6.72 us
    dot_general x2, matrix products, on_device(): jnp.dot(lax.all_gather(xb, 'col', axis=1, tiled=True), x_panel, preferred...  6.54 us
    dot_general x2, matrix products, on_device(): jnp.dot(lax.all_gather(xb, 'col', axis=1, tiled=True), q_panel, preferred...  5.63 us
  transfers between devices with their start and end apart: 8, of which 8 were waited for; matrix products, arithmetic and copies ran while one was open for 3% of the time, Pallas kernels for 0%

commit v1 on v0

--- a/solution.py
+++ b/solution.py
@@ -41,7 +41,14 @@
         )
         square = apply_mask(square, blocks)
         qb = square.astype(jnp.bfloat16)
-        q_panel = lax.all_gather(qb, "row", axis=0, tiled=True)
+        ring = [qb]
+        for hop in range(3):
+            ring.append(lax.ppermute(ring[-1], "row", [(dev, (dev + 1) % 4) for dev in range(4)]))
+        q_panel = jnp.roll(
+            jnp.concatenate(ring[::-1], axis=0),
+            (lax.axis_index("row") + 1) * ring[0].shape[0],
+            axis=0,
+        )
         total = jnp.dot(
             lax.all_gather(qb, "col", axis=1, tiled=True),
             x_panel,

time: 266 us -> 222 us (0.83)
  waiting for transfers between devices: 229 us -> 176 us
  matrix products: 18.9 us -> 23.3 us
  starting transfers between devices: 0.28 us -> 3.32 us
    all_gather x2 -> x0, waiting for transfers between devices: 48.3 us -> none  [on_device(): q_panel = lax.all_gather(qb, 'row', axis=0, tiled=True)]
    all_gather x2, waiting for transfers between devices: 58.7 us -> 22.5 us  [on_device(): lax.all_gather(qb, 'col', axis=1, tiled=True)]
    ppermute x0 -> x6, waiting for transfers between devices: none -> 33.7 us  [on_device(): lax.ppermute(ring[-1], 'row', [(dev, (dev + 1) % 4) for dev in range(4)])]
    dot_general x2, matrix products: 5.63 us -> 11.6 us  [on_device(): jnp.dot(lax.all_gather(xb, 'col', axis=1, tiled=True), q_panel, preferred...]
    ppermute x0 -> x6, starting transfers between devices: none -> 3.12 us  [on_device(): lax.ppermute(ring[-1], 'row', [(dev, (dev + 1) % 4) for dev in range(4)])]
  transfers between devices with their start and end apart: 8 -> 12, of which waited for: 8 -> 10; matrix products, arithmetic and copies ran while one was open for 3% -> 2% of each run, Pallas kernels for 0% -> 0%
where the time goes in v1:
time: 222 us; the launch traced here: 221 us
  waiting for transfers between devices  176 us (79%)
  matrix products  23.3 us (10%)
  between operations  13.6 us (6%)
  starting transfers between devices  3.32 us (1%)
  other arithmetic  2.56 us (1%)
    all_gather x2, waiting for transfers between devices, on_device(): lax.all_gather(xb, 'col', axis=1, tiled=True)  64.8 us
    all_gather x2, waiting for transfers between devices, on_device(): x_panel = lax.all_gather(xb, 'row', axis=0, tiled=True)  53.9 us
    ppermute x6, waiting for transfers between devices, on_device(): lax.ppermute(ring[-1], 'row', [(dev, (dev + 1) % 4) for dev in range(4)])  33.7 us
    all_gather x2, waiting for transfers between devices, on_device(): lax.all_gather(qb, 'col', axis=1, tiled=True)  22.5 us
    dot_general x2, matrix products, on_device(): jnp.dot(lax.all_gather(xb, 'col', axis=1, tiled=True), q_panel, preferred...  11.6 us
    dot_general x2, matrix products, on_device(): jnp.dot(lax.all_gather(xb, 'col', axis=1, tiled=True), x_panel, preferred...  6.54 us
    dot_general x2, matrix products, on_device(): jnp.dot(lax.all_gather(qb, 'col', axis=1, tiled=True), x_panel, preferred...  5.17 us
  transfers between devices with their start and end apart: 12, of which 10 were waited for; matrix products, arithmetic and copies ran while one was open for 2% of the time, Pallas kernels for 0%

profile of v1, /device:TPU:0, one launch (start us, length us, event | category | flops | bytes accessed | tf_op | source)
XLA Modules:
  0.0 220.7 jit_solution(3040856567917370889)
XLA Ops:
  6.5 0.8 copy.3
  7.3 0.8 fusion.27
  8.3 1.8 fusion.23
  10.2 0.7 all-gather.7.cloned.1.call-update
  10.9 28.7 %all-gather.9.cloned.1.call-done = bf16[2048,256]{1,0:T(8,128)(2,1)} async-done(((bf16[512,256]{1,0:T(8,128)(2,1)}), bf16[2048,256]{1,0:T(8,128)(2,1)}) %all-gather.9.cloned.1.call-update) | async-done | bytes 1048592 | tf_op jit(solution)/shard_map/all_gather | solution.py:36
  39.6 32.5 %all-gather.7.cloned.1.call-done = bf16[512,2048]{1,0:T(8,128)(2,1)} async-done(((bf16[512,256]{1,0:T(8,128)(2,1)}), bf16[512,2048]{1,0:T(8,128)(2,1)}) %all-gather.7.cloned.1.call-update) | async-done | bytes 2097168 | tf_op jit(solution)/shard_map/all_gather | solution.py:38
  72.0 3.3 %fusion.30 = (bf16[512,256]{1,0:T(8,128)(2,1)}, f32[512,256]{1,0:T(8,128)S(1)}) fusion(f32[64,8,2,128]{3,2,1,0:T(2,128)S(1)} %bitcast.22, bf16[512,2048]{1,0:T(8,128)(2,1)} %all-gather.7.cloned.1.call-done, bf16[2048,256]{1,0:T(8,128)(2,1)} %all-gather.9.cloned.1.call-done), kind=kOutput, calls=%fused_computation.49 | convolution fusion | flops 537133056 | bytes 4456448 | tf_op jit(solution)/shard_map/dot_general | solution.py:37
  75.4 1.3 collective-permute-start
  76.6 8.5 %collective-permute-done = bf16[512,256]{1,0:T(8,128)(2,1)} collective-permute-done((bf16[512,256]{1,0:T(8,128)(2,1)}, bf16[512,256]{1,0:T(8,128)(2,1)}, u32[]{:S(2)}, u32[]{:S(2)}) %collective-permute-start) | collective-permute-done | bytes 262176 | tf_op jit(solution)/shard_map/ppermute | solution.py:46
  85.4 8.6 %collective-permute-done.1 = bf16[512,256]{1,0:T(8,128)(2,1)} collective-permute-done((bf16[512,256]{1,0:T(8,128)(2,1)}, bf16[512,256]{1,0:T(8,128)(2,1)}, u32[]{:S(2)}, u32[]{:S(2)}) %collective-permute-start.1) | collective-permute-done | bytes 262176 | tf_op jit(solution)/shard_map/ppermute | solution.py:46
  94.0 11.4 %all-gather.11.cloned.1.call-done = bf16[512,2048]{1,0:T(8,128)(2,1)} async-done(((bf16[512,256]{1,0:T(8,128)(2,1)}), bf16[512,2048]{1,0:T(8,128)(2,1)}) %all-gather.11.cloned.1.call-update) | async-done | bytes 2097168 | tf_op jit(solution)/shard_map/all_gather | solution.py:53
  105.4 2.6 %fusion.32 = f32[512,256]{1,0:T(8,128)S(1)} fusion(bf16[512,2048]{1,0:T(8,128)(2,1)} %all-gather.11.cloned.1.call-done, bf16[2048,256]{1,0:T(8,128)(2,1)} %all-gather.9.cloned.1.call-done), kind=kOutput, calls=%fused_computation.51 | convolution fusion | flops 536870912 | bytes 3670016 | tf_op jit(solution)/shard_map/dot_general | solution.py:52
  108.0 5.0 %fusion.4 = bf16[512,256]{1,0:T(8,128)(2,1)} fusion(f32[512,256]{1,0:T(8,128)S(1)} %fusion.32, bf16[512,2048]{1,0:T(8,128)(2,1)S(1)} %copy-done, s32[]{:T(128)S(6)} %select_n.21, bf16[512,256]{1,0:T(8,128)(2,1)} %collective-permute-done.2, bf16[512,256]{1,0:T(8,128)(2,1)} %collective-permute-done.1, bf16[512,256]{1,0:T(8,128)(2,1)} %collective-permute-done, ...), kind=kOutput, calls=%fused_computation.24 | convolution fusion | flops 545914880 | bytes 4980740 | tf_op jit(solution)/shard_map/dot_general | solution.py:57
  113.1 0.5 all-gather.13.cloned.1.call-update
  113.6 25.2 %all-gather.15.cloned.1.call-done = bf16[2048,256]{1,0:T(8,128)(2,1)} async-done(((bf16[512,256]{1,0:T(8,128)(2,1)}), bf16[2048,256]{1,0:T(8,128)(2,1)}) %all-gather.15.cloned.1.call-update) | async-done | bytes 1048592 | tf_op jit(solution)/shard_map/all_gather | solution.py:36
  138.9 32.3 %all-gather.13.cloned.1.call-done = bf16[512,2048]{1,0:T(8,128)(2,1)} async-done(((bf16[512,256]{1,0:T(8,128)(2,1)}), bf16[512,2048]{1,0:T(8,128)(2,1)}) %all-gather.13.cloned.1.call-update) | async-done | bytes 2097168 | tf_op jit(solution)/shard_map/all_gather | solution.py:38
  171.2 3.3 %fusion.31 = (bf16[512,256]{1,0:T(8,128)(2,1)}, f32[512,256]{1,0:T(8,128)S(1)}) fusion(f32[64,8,2,128]{3,2,1,0:T(2,128)S(1)} %bitcast.24, bf16[512,2048]{1,0:T(8,128)(2,1)} %all-gather.13.cloned.1.call-done, bf16[2048,256]{1,0:T(8,128)(2,1)} %all-gather.15.cloned.1.call-done), kind=kOutput, calls=%fused_computation.50 | convolution fusion | flops 537133056 | bytes 4456448 | tf_op jit(solution)/shard_map/dot_general | solution.py:37
  174.5 1.3 collective-permute-start.3
  175.7 8.4 %collective-permute-done.3 = bf16[512,256]{1,0:T(8,128)(2,1)S(1)} collective-permute-done((bf16[512,256]{1,0:T(8,128)(2,1)}, bf16[512,256]{1,0:T(8,128)(2,1)S(1)}, u32[]{:S(2)}, u32[]{:S(2)}) %collective-permute-start.3) | collective-permute-done | bytes 262176 | tf_op jit(solution)/shard_map/ppermute | solution.py:46
  184.1 0.7 copy-done.4
  185.1 8.3 %collective-permute-done.4 = bf16[512,256]{1,0:T(8,128)(2,1)} collective-permute-done((bf16[512,256]{1,0:T(8,128)(2,1)S(1)}, bf16[512,256]{1,0:T(8,128)(2,1)}, u32[]{:S(2)}, u32[]{:S(2)}) %collective-permute-start.4) | collective-permute-done | bytes 262176 | tf_op jit(solution)/shard_map/ppermute | solution.py:46
  193.4 11.1 %all-gather.17.cloned.1.call-done = bf16[512,2048]{1,0:T(8,128)(2,1)} async-done(((bf16[512,256]{1,0:T(8,128)(2,1)}), bf16[512,2048]{1,0:T(8,128)(2,1)}) %all-gather.17.cloned.1.call-update) | async-done | bytes 2097168 | tf_op jit(solution)/shard_map/all_gather | solution.py:53
  204.5 2.6 %fusion.33 = f32[512,256]{1,0:T(8,128)S(1)} fusion(bf16[512,2048]{1,0:T(8,128)(2,1)} %all-gather.17.cloned.1.call-done, bf16[2048,256]{1,0:T(8,128)(2,1)} %all-gather.15.cloned.1.call-done), kind=kOutput, calls=%fused_computation.52 | convolution fusion | flops 536870912 | bytes 3670016 | tf_op jit(solution)/shard_map/dot_general | solution.py:52
  207.2 6.6 %fusion.3 = f32[512,256]{1,0:T(8,128)} fusion(f32[512,256]{1,0:T(8,128)S(1)} %fusion.33, bf16[512,2048]{1,0:T(8,128)(2,1)S(1)} %copy-done.1, s32[]{:T(128)S(6)} %select_n.21, bf16[512,256]{1,0:T(8,128)(2,1)} %collective-permute-done.5, bf16[512,256]{1,0:T(8,128)(2,1)} %collective-permute-done.4, bf16[512,256]{1,0:T(8,128)(2,1)S(1)} %copy-done.5, ...), kind=kOutput, calls=%fused_computation.23 | convolution fusion | flops 545783808 | bytes 5242884 | tf_op jit(solution)/shard_map/dot_general | solution.py:57
  (28 shorter events, 1.1 us)
Async XLA Ops:
  6.5 33.0 %all-gather.9.cloned.1.call-start = ((), (), s32[]{:S(2)}) async-start(), calls=%async_computation.1 | async-start | bytes 1310720 | tf_op jit(solution)/shard_map/all_gather | solution.py:36
  10.1 61.9 %all-gather.7.cloned.1.call-start = ((), (), s32[]{:S(2)}) async-start(), calls=%async_computation | async-start | bytes 2359296 | tf_op jit(solution)/shard_map/all_gather | solution.py:38
  10.9 94.5 %all-gather.11.cloned.1.call-start = ((), (), s32[]{:S(2)}) async-start(), calls=%async_computation.2 | async-start | bytes 2359296 | tf_op jit(solution)/shard_map/all_gather | solution.py:53
  75.3 32.7 %copy-start = (bf16[512,2048]{1,0:T(8,128)(2,1)S(1)}, bf16[512,2048]{1,0:T(8,128)(2,1)}, u32[]{:S(2)}) copy-start(bf16[512,2048]{1,0:T(8,128)(2,1)} %all-gather.7.cloned.1.call-done) | copy-start | bytes 6291460
  75.3 32.7 %copy-start.2 = (bf16[512,256]{1,0:T(8,128)(2,1)S(1)}, bf16[512,256]{1,0:T(8,128)(2,1)}, u32[]{:S(2)}) copy-start(bf16[512,256]{1,0:T(8,128)(2,1)} %get-tuple-element.6) | copy-start | bytes 786436
  75.3 63.5 %all-gather.15.cloned.1.call-start = ((), (), s32[]{:S(2)}) async-start(), calls=%async_computation.4 | async-start | bytes 1310720 | tf_op jit(solution)/shard_map/all_gather | solution.py:36
  75.4 9.7 %collective-permute-start = (bf16[512,256]{1,0:T(8,128)(2,1)}, bf16[512,256]{1,0:T(8,128)(2,1)}, u32[]{:S(2)}, u32[]{:S(2)}) collective-permute-start(bf16[512,256]{1,0:T(8,128)(2,1)} %get-tuple-element.6), channel_id=1, source_target_pairs={{0,8},{8,16},{16,24},{24,0},{1,9},{9,17},{17,25},{25,1},{2,10},{10... | collective-permute-start | bytes 786440 | tf_op jit(solution)/shard_map/ppermute | solution.py:46
  85.1 8.9 %collective-permute-start.1 = (bf16[512,256]{1,0:T(8,128)(2,1)}, bf16[512,256]{1,0:T(8,128)(2,1)}, u32[]{:S(2)}, u32[]{:S(2)}) collective-permute-start(bf16[512,256]{1,0:T(8,128)(2,1)} %collective-permute-done), channel_id=1, source_target_pairs={{0,8},{8,16},{16,24},{24,0},{1,9},{9,17},{17,25},{25,1},{2,10},{10... | collective-permute-start | bytes 786440 | tf_op jit(solution)/shard_map/ppermute | solution.py:46
  94.0 14.0 %collective-permute-start.2 = (bf16[512,256]{1,0:T(8,128)(2,1)}, bf16[512,256]{1,0:T(8,128)(2,1)}, u32[]{:S(2)}, u32[]{:S(2)}) collective-permute-start(bf16[512,256]{1,0:T(8,128)(2,1)} %collective-permute-done.1), channel_id=1, source_target_pairs={{0,8},{8,16},{16,24},{24,0},{1,9},{9,17},{17,25},{25,1},{2,10},{10... | collective-permute-start | bytes 786440 | tf_op jit(solution)/shard_map/ppermute | solution.py:46
  113.0 58.2 %all-gather.13.cloned.1.call-start = ((), (), s32[]{:S(2)}) async-start(), calls=%async_computation.3 | async-start | bytes 2359296 | tf_op jit(solution)/shard_map/all_gather | solution.py:38
  113.6 90.9 %all-gather.17.cloned.1.call-start = ((), (), s32[]{:S(2)}) async-start(), calls=%async_computation.5 | async-start | bytes 2359296 | tf_op jit(solution)/shard_map/all_gather | solution.py:53
  174.4 32.7 %copy-start.1 = (bf16[512,2048]{1,0:T(8,128)(2,1)S(1)}, bf16[512,2048]{1,0:T(8,128)(2,1)}, u32[]{:S(2)}) copy-start(bf16[512,2048]{1,0:T(8,128)(2,1)} %all-gather.13.cloned.1.call-done) | copy-start | bytes 6291460
  174.4 32.7 %copy-start.3 = (bf16[512,256]{1,0:T(8,128)(2,1)S(1)}, bf16[512,256]{1,0:T(8,128)(2,1)}, u32[]{:S(2)}) copy-start(bf16[512,256]{1,0:T(8,128)(2,1)} %get-tuple-element.8) | copy-start | bytes 786436
  174.5 9.6 %collective-permute-start.3 = (bf16[512,256]{1,0:T(8,128)(2,1)}, bf16[512,256]{1,0:T(8,128)(2,1)S(1)}, u32[]{:S(2)}, u32[]{:S(2)}) collective-permute-start(bf16[512,256]{1,0:T(8,128)(2,1)} %get-tuple-element.8), channel_id=1, source_target_pairs={{0,8},{8,16},{16,24},{24,0},{1,9},{9,17},{17,25},{25,1},{2,10},{10... | collective-permute-start | bytes 786440 | tf_op jit(solution)/shard_map/ppermute | solution.py:46
  184.1 0.7 copy-start.4
  184.8 8.7 %collective-permute-start.4 = (bf16[512,256]{1,0:T(8,128)(2,1)S(1)}, bf16[512,256]{1,0:T(8,128)(2,1)}, u32[]{:S(2)}, u32[]{:S(2)}) collective-permute-start(bf16[512,256]{1,0:T(8,128)(2,1)S(1)} %collective-permute-done.3), channel_id=1, source_target_pairs={{0,8},{8,16},{16,24},{24,0},{1,9},{9,17},{17,25},{25,1},{2,10},{10... | collective-permute-start | bytes 786440 | tf_op jit(solution)/shard_map/ppermute | solution.py:46
  193.4 13.7 %collective-permute-start.5 = (bf16[512,256]{1,0:T(8,128)(2,1)}, bf16[512,256]{1,0:T(8,128)(2,1)}, u32[]{:S(2)}, u32[]{:S(2)}) collective-permute-start(bf16[512,256]{1,0:T(8,128)(2,1)} %collective-permute-done.4), channel_id=1, source_target_pairs={{0,8},{8,16},{16,24},{24,0},{1,9},{9,17},{17,25},{25,1},{2,10},{10... | collective-permute-start | bytes 786440 | tf_op jit(solution)/shard_map/ppermute | solution.py:46
  204.5 2.6 %copy-start.5 = (bf16[512,256]{1,0:T(8,128)(2,1)S(1)}, bf16[512,256]{1,0:T(8,128)(2,1)}, u32[]{:S(2)}) copy-start(bf16[512,256]{1,0:T(8,128)(2,1)} %copy-done.4) | copy-start | bytes 786436
Sparse Core Ops, SparseCore 0:
  10.2 29.3 all-gather.8
  41.2 30.8 all-gather.6
  75.5 29.8 all-gather.10
  113.1 25.6 all-gather.14
  140.3 30.8 all-gather.12
  174.6 29.8 all-gather.16
